TPU v7x, 256 devices: a whole 4x4x8 slice. The times are simulated.
256 devices in a mesh: row: 8 (over x, core), col: 32 (over y, z).
Axes of the slice: x: 4, y: 4, z: 8, core: 2. Of those that a mesh axis runs over, the one named last changes fastest.
Arguments:
- tokens: bfloat16 [512, 8192], P('col', 'row'), may hold values from -6 to 6
- cotangent: bfloat16 [512, 8192], P('col', 'row'), may hold values from -6 to 6
- gate_weight: bfloat16 [8192, 28672], P('row', 'col'), may hold values from -0.09375 to 0.09375
- up_weight: bfloat16 [8192, 28672], P('row', 'col'), may hold values from -0.09375 to 0.09375
- down_weight: bfloat16 [28672, 8192], P('col', 'row'), may hold values from -0.046875 to 0.046875
- block_mask: int32 [3, 64, 224], P(None, 'row', 'col'), may hold values 0 or 1
Outputs:
- layer_out: bfloat16 [512, 8192], P('col', 'row')
- token_grad: bfloat16 [512, 8192], P('col', 'row')
- gate_grad: bfloat16 [8192, 28672], P('row', 'col')
- up_grad: bfloat16 [8192, 28672], P('row', 'col')
- down_grad: bfloat16 [28672, 8192], P('col', 'row')
All inputs are finite; a program needn't handle non-finite values. No bound on the sum of `block_mask` on one device may be relied on, other than what follows from the above.
Results may differ from a plain program's by a relative error of at most 0.025.
Values may be sent and summed in bfloat16 or wider, within the bound.
No kernel may reach another device: no remote copies, remote signals or barrier semaphores. Data moves between devices by JAX's collectives and lax.ppermute only.
A program may use at most 64 MiB of HBM per device.

v0:
```python
import jax
import jax.numpy as jnp
from jax import lax
from jax.sharding import PartitionSpec as P


def masked(weight, mask):
    rows, cols = mask.shape
    shaped = weight.reshape(rows, weight.shape[0] // rows, cols, weight.shape[1] // cols)
    return (shaped * mask.astype(weight.dtype)[:, None, :, None]).reshape(weight.shape)


def product(left, weight):
    return jnp.dot(left, weight, preferred_element_type=jnp.float32)


def product_t(left, weight):
    return lax.dot_general(
        left, weight, (((1,), (1,)), ((), ())), preferred_element_type=jnp.float32
    )


def contract_rows(left, right):
    return lax.dot_general(
        left, right, (((0,), (0,)), ((), ())), preferred_element_type=jnp.float32
    )


def gather_rows(local, axis, size):
    sent = jnp.broadcast_to(local[None], (size,) + local.shape)
    got = lax.all_to_all(sent, axis, 0, 0, tiled=False)
    return got.reshape((size * local.shape[0],) + local.shape[1:])


def reduce_rows(partial, axis, size):
    chunks = partial.astype(jnp.bfloat16).reshape(
        (size, partial.shape[0] // size) + partial.shape[1:]
    )
    got = lax.all_to_all(chunks, axis, 0, 0, tiled=False)
    return got.astype(jnp.float32).sum(axis=0)


def shards(tokens, cotangent, gate_weight, up_weight, down_weight, block_mask):
    n_row = lax.axis_size("row")
    n_col = lax.axis_size("col")
    masked_gate = masked(gate_weight, block_mask[0])
    masked_up = masked(up_weight, block_mask[1])
    masked_down = masked(down_weight, block_mask[2].T)
    feat = tokens.shape[1]
    panel = gather_rows(tokens, "col", n_col)
    grad_panel = gather_rows(cotangent, "col", n_col)
    total_rows = panel.shape[0]
    width = masked_gate.shape[1]
    fwd = reduce_rows(
        jnp.concatenate(
            [
                product(panel, masked_gate).astype(jnp.bfloat16),
                product(panel, masked_up).astype(jnp.bfloat16),
            ],
            axis=1,
        ),
        "row",
        n_row,
    )
    gate = fwd[:, :width]
    up = fwd[:, width:]
    sigma = jax.nn.sigmoid(gate)
    act = (gate * sigma * up).astype(jnp.bfloat16)
    act_full = lax.all_gather(act, "row", axis=0, tiled=True)
    layer_out = reduce_rows(product(act_full, masked_down), "col", n_col).astype(jnp.bfloat16)
    dact = reduce_rows(product_t(grad_panel, masked_down), "row", n_row)
    dgate = (dact * up * sigma * (1.0 + gate * (1.0 - sigma))).astype(jnp.bfloat16)
    dup = (dact * gate * sigma).astype(jnp.bfloat16)
    full = lax.all_gather(jnp.concatenate([dgate, dup], axis=1), "row", axis=0, tiled=True)
    dgate_full = full[:, :width]
    dup_full = full[:, width:]
    token_grad = reduce_rows(
        product_t(dgate_full, masked_gate) + product_t(dup_full, masked_up), "col", n_col
    ).astype(jnp.bfloat16)
    scale = total_rows ** (-0.5)
    gate_grad = masked(contract_rows(panel, dgate_full) * scale, block_mask[0]).astype(jnp.bfloat16)
    up_grad = masked(contract_rows(panel, dup_full) * scale, block_mask[1]).astype(jnp.bfloat16)
    down_grad = masked(contract_rows(act_full, grad_panel) * scale, block_mask[2].T).astype(
        jnp.bfloat16
    )
    return (layer_out, token_grad, gate_grad, up_grad, down_grad)


def solution(mesh):
    in_specs = (
        P("col", "row"),
        P("col", "row"),
        P("row", "col"),
        P("row", "col"),
        P("col", "row"),
        P(None, "row", "col"),
    )
    out_specs = (
        P("col", "row"),
        P("col", "row"),
        P("row", "col"),
        P("row", "col"),
        P("col", "row"),
    )
    return jax.shard_map(shards, mesh=mesh, in_specs=in_specs, out_specs=out_specs, check_vma=False)
```

profile of v0, /device:TPU:32, one launch (start us, length us, event | category | flops | bytes accessed | tf_op | source)
XLA Modules:
  0.0 223.7 jit_solution(11346078941495549265)
XLA Ops:
  7.2 0.9 broadcast_in_dim.5
  8.1 39.7 %all_to_all.30 = bf16[32,16,1024]{2,1,0:T(8,128)(2,1)S(1)} all-to-all(bf16[32,16,1024]{2,1,0:T(8,128)(2,1)S(1)} %broadcast_in_dim.5), channel_id=1, replica_groups=mesh['row'=8,'col'=32] {'col'}, dimensions={0} | all-to-all | bytes 2097152 | tf_op jit(solution)/shard_map/all_to_all | solution.py:31
  47.7 1.1 broadcast_in_dim.4
  48.8 5.3 %all-to-all-start = ((bf16[32,16,1024]{2,1,0:T(8,128)(2,1)}), bf16[32,16,1024]{2,1,0:T(8,128)(2,1)}, u32[]{:S(2)}, u32[]{:S(2)}) async-start(bf16[32,16,1024]{2,1,0:T(8,128)(2,1)} %broadcast_in_dim.4), calls=%async_computation | async-start | bytes 2097152 | tf_op jit(solution)/shard_map/all_to_all | solution.py:31
  54.2 2.4 %copy.20 = bf16[1024,896]{0,1:T(8,128)(2,1)} copy(bf16[1024,896]{1,0:T(8,128)(2,1)S(1)} %copy-done.2) | data formatting | bytes 3670016 | tf_op args[3]
  56.7 3.8 %copy.18 = bf16[1024,896]{0,1:T(8,128)(2,1)} copy(bf16[1024,896]{1,0:T(8,128)(2,1)} %param.8) | data formatting | bytes 3670016 | tf_op args[2]
  60.6 0.3 mul.114
  60.9 1.2 copy-done.8
  62.1 0.2 copy-done.13
  62.3 2.3 %convolution_convert_fusion.1 = bf16[896,512]{0,1:T(8,128)(2,1)} fusion(bf16[512,1024]{1,0:T(8,128)(2,1)S(1)} %bitcast.85, bf16[896,1024]{1,0:T(8,128)(2,1)S(1)} %copy-done.13, bf16[112,8,8,128]{3,2,1,0:T(8,128)(2,1)S(1)} %bitcast.91), kind=kOutput, calls=%fused_computation.14 | convolution fusion | flops 940900352 | bytes 5636096 | tf_op jit(solution)/shard_map/dot_general | solution.py:18
  64.5 17.6 %all-to-all-done = bf16[32,16,1024]{2,1,0:T(8,128)(2,1)} async-done(((bf16[32,16,1024]{2,1,0:T(8,128)(2,1)}), bf16[32,16,1024]{2,1,0:T(8,128)(2,1)}, u32[]{:S(2)}, u32[]{:S(2)}) %all-to-all-start) | async-done | bytes 1048608 | tf_op jit(solution)/shard_map/all_to_all | solution.py:31
  82.2 4.4 %all-to-all-start.4 = ((bf16[8,64,896]{2,1,0:T(8,128)(2,1)}), bf16[8,64,896]{2,1,0:T(8,128)(2,1)}, u32[]{:S(2)}, u32[]{:S(2)}) async-start(bf16[8,64,896]{2,1,0:T(8,128)(2,1)} %bitcast.97), calls=%async_computation.4 | async-start | bytes 1835008 | tf_op jit(solution)/shard_map/all_to_all | solution.py:39
  86.6 0.3 mul.109
  86.9 1.2 copy-done.6
  88.1 2.4 %fusion.4 = bf16[512,896]{0,1:T(8,128)(2,1)S(1)} fusion(bf16[512,1024]{1,0:T(8,128)(2,1)} %bitcast.1, bf16[1024,896]{0,1:T(8,128)(2,1)S(1)} %copy-done.3, bf16[112,8,8,128]{3,2,1,0:T(8,128)(2,1)S(1)} %bitcast.89), kind=kOutput, calls=%fused_computation.18 | convolution fusion | flops 940900352 | bytes 5636096 | tf_op jit(solution)/shard_map/dot_general | solution.py:14
  90.5 0.3 mul.106
  90.9 1.7 copy-done.5
  92.6 2.4 %fusion.3 = bf16[512,896]{0,1:T(8,128)(2,1)S(1)} fusion(bf16[512,1024]{1,0:T(8,128)(2,1)} %bitcast.1, bf16[1024,896]{0,1:T(8,128)(2,1)S(1)} %copy-done.5, bf16[112,8,8,128]{3,2,1,0:T(8,128)(2,1)S(1)} %bitcast.93), kind=kOutput, calls=%fused_computation.17 | convolution fusion | flops 940900352 | bytes 5636096 | tf_op jit(solution)/shard_map/dot_general | solution.py:14
  95.1 2.4 %copy.21 = bf16[512,1792]{1,0:T(8,128)(2,1)} copy(bf16[512,1792]{0,1:T(8,128)(2,1)S(1)} %pad_maximum_fusion) | data formatting | bytes 3670016 | tf_op jit(solution)/shard_map/concatenate | solution.py:55
  97.5 3.8 %all-to-all-done.4 = bf16[8,64,896]{2,1,0:T(8,128)(2,1)} async-done(((bf16[8,64,896]{2,1,0:T(8,128)(2,1)}), bf16[8,64,896]{2,1,0:T(8,128)(2,1)}, u32[]{:S(2)}, u32[]{:S(2)}) %all-to-all-start.4) | async-done | bytes 917536 | tf_op jit(solution)/shard_map/all_to_all | solution.py:39
  101.2 3.6 %all-to-all-start.1 = ((bf16[8,64,1792]{2,1,0:T(8,128)(2,1)}), bf16[8,64,1792]{2,1,0:T(8,128)(2,1)S(1)}, u32[]{:S(2)}, u32[]{:S(2)}) async-start(bf16[8,64,1792]{2,1,0:T(8,128)(2,1)} %bitcast.5), calls=%async_computation.1 | async-start | bytes 3670016 | tf_op jit(solution)/shard_map/all_to_all | solution.py:39
  104.9 1.3 convert_reduce_fusion.1
  106.2 22.9 %all-to-all-done.1 = bf16[8,64,1792]{2,1,0:T(8,128)(2,1)S(1)} async-done(((bf16[8,64,1792]{2,1,0:T(8,128)(2,1)}), bf16[8,64,1792]{2,1,0:T(8,128)(2,1)S(1)}, u32[]{:S(2)}, u32[]{:S(2)}) %all-to-all-start.1) | async-done | bytes 1835040 | tf_op jit(solution)/shard_map/all_to_all | solution.py:39
  129.1 0.2 convert_reduce_fusion
  129.4 0.2 multiply_convert_fusion.1
  129.5 0.7 pad_maximum_fusion.1
  130.3 14.7 %all_gather.6 = bf16[512,896]{1,0:T(8,128)(2,1)S(1)} all-gather(bf16[64,896]{1,0:T(8,128)(2,1)S(1)} %get-tuple-element.17), channel_id=1, replica_groups=mesh['row'=8,'col'=32] {'row'}, dimensions={0}, use_global_device_ids=true | all-gather | bytes 1032192 | tf_op jit(solution)/shard_map/all_gather | solution.py:69
  145.0 4.1 %convolution_convert_fusion = bf16[512,1024]{1,0:T(8,128)(2,1)} fusion(bf16[512,896]{1,0:T(8,128)(2,1)S(1)} %all_gather.6, bf16[896,1024]{1,0:T(8,128)(2,1)} %param.10, bf16[112,8,8,128]{3,2,1,0:T(8,128)(2,1)S(1)} %bitcast.92), kind=kOutput, calls=%fused_computation.13 | convolution fusion | flops 940965888 | bytes 5636096 | tf_op jit(solution)/shard_map/dot_general | solution.py:14
  149.2 4.3 %all-to-all-start.2 = ((bf16[32,16,1024]{2,1,0:T(8,128)(2,1)}), bf16[32,16,1024]{2,1,0:T(8,128)(2,1)S(1)}, u32[]{:S(2)}, u32[]{:S(2)}) async-start(bf16[32,16,1024]{2,1,0:T(8,128)(2,1)} %bitcast.96), calls=%async_computation.2 | async-start | bytes 2097152 | tf_op jit(solution)/shard_map/all_to_all | solution.py:39
  153.5 3.7 %fusion.8 = f32[512,1024]{1,0:T(8,128)S(1)} fusion(bf16[512,1792]{1,0:T(8,128)(2,1)} %all-gather.2.cloned.1.call-done, bf16[1024,896]{0,1:T(8,128)(2,1)} %copy.18, bf16[112,8,8,128]{3,2,1,0:T(8,128)(2,1)} %bitcast.94), kind=kOutput, calls=%fused_computation.22 | convolution fusion | flops 940441600 | bytes 6684672 | tf_op jit(solution)/shard_map/dot_general | solution.py:18
  157.3 0.2 copy-done.14
  157.5 2.2 %add_convert_fusion = bf16[512,1024]{1,0:T(8,128)(2,1)} fusion(f32[512,1024]{1,0:T(8,128)S(1)} %fusion.8, bf16[512,1792]{1,0:T(8,128)(2,1)S(1)} %copy-done.14, bf16[1024,896]{0,1:T(8,128)(2,1)S(1)} %copy-done.4, bf16[112,8,8,128]{3,2,1,0:T(8,128)(2,1)S(1)} %bitcast.90), kind=kOutput, calls=%fused_computation.7 | convolution fusion | flops 941490176 | bytes 7733248 | tf_op jit(solution)/shard_map/dot_general | solution.py:18
  159.7 22.5 %all-to-all-done.2 = bf16[32,16,1024]{2,1,0:T(8,128)(2,1)S(1)} async-done(((bf16[32,16,1024]{2,1,0:T(8,128)(2,1)}), bf16[32,16,1024]{2,1,0:T(8,128)(2,1)S(1)}, u32[]{:S(2)}, u32[]{:S(2)}) %all-to-all-start.2) | async-done | bytes 1048608 | tf_op jit(solution)/shard_map/all_to_all | solution.py:39
  182.2 5.6 %all-to-all-start.5 = ((bf16[32,16,1024]{2,1,0:T(8,128)(2,1)}), bf16[32,16,1024]{2,1,0:T(8,128)(2,1)S(1)}, u32[]{:S(2)}, u32[]{:S(2)}) async-start(bf16[32,16,1024]{2,1,0:T(8,128)(2,1)} %bitcast.95), calls=%async_computation.5 | async-start | bytes 2097152 | tf_op jit(solution)/shard_map/all_to_all | solution.py:39
  188.1 0.3 mul.134
  188.4 0.9 copy-done.1
  189.3 2.8 %fusion = bf16[896,1024]{1,0:T(8,128)(2,1)} fusion(f32[112,8,8,128]{3,2,1,0:T(8,128)S(1)} %bitcast.84, bf16[512,896]{1,0:T(8,128)(2,1)S(1)} %copy-done.1, bf16[512,1024]{1,0:T(8,128)(2,1)S(1)} %bitcast.86), kind=kOutput, calls=%fused_computation.1 | convolution fusion | flops 942276608 | bytes 7471104 | tf_op jit(solution)/shard_map/dot_general | solution.py:24
  192.1 0.8 reduce_sum.43
  192.9 0.3 mul.125
  193.2 1.2 copy-done.15
  194.4 4.0 %fusion.2 = bf16[1024,896]{0,1:T(8,128)(2,1)} fusion(f32[112,8,8,128]{3,2,1,0:T(8,128)S(1)} %bitcast.88, bf16[512,1024]{1,0:T(8,128)(2,1)} %bitcast.1, bf16[512,1792]{1,0:T(8,128)(2,1)S(1)} %copy-done.15), kind=kOutput, calls=%fused_computation.5 | convolution fusion | flops 942276608 | bytes 7471104 | tf_op jit(solution)/shard_map/dot_general | solution.py:24
  198.4 3.8 %copy.26 = bf16[1024,896]{1,0:T(8,128)(2,1)} copy(bf16[1024,896]{0,1:T(8,128)(2,1)} %fusion.2) | data formatting | bytes 3670016
  202.2 0.3 mul.130
  202.5 1.2 copy-done.16
  203.7 4.0 %fusion.1 = bf16[1024,896]{0,1:T(8,128)(2,1)} fusion(f32[112,8,8,128]{3,2,1,0:T(8,128)S(1)} %bitcast.87, bf16[512,1024]{1,0:T(8,128)(2,1)} %bitcast.1, bf16[512,1792]{1,0:T(8,128)(2,1)S(1)} %copy-done.16), kind=kOutput, calls=%fused_computation.3 | convolution fusion | flops 942276608 | bytes 7471104 | tf_op jit(solution)/shard_map/dot_general | solution.py:24
  207.7 3.8 %copy.27 = bf16[1024,896]{1,0:T(8,128)(2,1)} copy(bf16[1024,896]{0,1:T(8,128)(2,1)} %fusion.1) | data formatting | bytes 3670016
  211.5 4.6 %all-to-all-done.5 = bf16[32,16,1024]{2,1,0:T(8,128)(2,1)S(1)} async-done(((bf16[32,16,1024]{2,1,0:T(8,128)(2,1)}), bf16[32,16,1024]{2,1,0:T(8,128)(2,1)S(1)}, u32[]{:S(2)}, u32[]{:S(2)}) %all-to-all-start.5) | async-done | bytes 1048608 | tf_op jit(solution)/shard_map/all_to_all | solution.py:39
  216.1 0.8 reduce_sum.45
  (37 shorter events, 0.8 us)
Async XLA Ops:
  7.2 40.6 %copy-start.11 = (bf16[16,1024]{1,0:T(8,128)(2,1)S(1)}, bf16[16,1024]{1,0:T(8,128)(2,1)}, u32[]{:S(2)}) copy-start(bf16[16,1024]{1,0:T(8,128)(2,1)} %param.6) | copy-start | bytes 98308
  47.7 6.4 %copy-start.12 = (s32[3,8,7]{2,1,0:T(8,128)S(1)}, s32[3,8,7]{2,1,0:T(8,128)}, u32[]{:S(2)}) copy-start(s32[3,8,7]{2,1,0:T(8,128)} %param.11) | copy-start | bytes 2020
  47.7 6.5 %copy-start.2 = (bf16[1024,896]{1,0:T(8,128)(2,1)S(1)}, bf16[1024,896]{1,0:T(8,128)(2,1)}, u32[]{:S(2)}) copy-start(bf16[1024,896]{1,0:T(8,128)(2,1)} %param.9) | copy-start | bytes 5505028
  48.8 33.3 %all-to-all-start = ((bf16[32,16,1024]{2,1,0:T(8,128)(2,1)}), bf16[32,16,1024]{2,1,0:T(8,128)(2,1)}, u32[]{:S(2)}, u32[]{:S(2)}) async-start(bf16[32,16,1024]{2,1,0:T(8,128)(2,1)} %broadcast_in_dim.4), calls=%async_computation | async-start | bytes 2097152 | tf_op jit(solution)/shard_map/all_to_all | solution.py:31
  60.5 1.8 copy-start.13
  60.9 1.2 copy-start.8
  82.2 6.0 %copy-start.3 = (bf16[1024,896]{0,1:T(8,128)(2,1)S(1)}, bf16[1024,896]{0,1:T(8,128)(2,1)}, u32[]{:S(2)}) copy-start(bf16[1024,896]{0,1:T(8,128)(2,1)} %copy.20) | copy-start | bytes 5505028
  82.2 19.1 %all-to-all-start.4 = ((bf16[8,64,896]{2,1,0:T(8,128)(2,1)}), bf16[8,64,896]{2,1,0:T(8,128)(2,1)}, u32[]{:S(2)}, u32[]{:S(2)}) async-start(bf16[8,64,896]{2,1,0:T(8,128)(2,1)} %bitcast.97), calls=%async_computation.4 | async-start | bytes 1835008 | tf_op jit(solution)/shard_map/all_to_all | solution.py:39
  86.9 1.2 copy-start.6
  90.5 2.0 copy-start.5
  90.8 4.1 %copy-start.10 = (bf16[8,128,7,128]{1,0,3,2:T(8,128)(2,1)}, bf16[8,128,7,128]{1,0,3,2:T(8,128)(2,1)S(1)}, u32[]{:S(2)}) copy-start(bf16[8,128,7,128]{1,0,3,2:T(8,128)(2,1)S(1)} %mul.106) | copy-start | bytes 5505028
  101.2 27.9 %all-to-all-start.1 = ((bf16[8,64,1792]{2,1,0:T(8,128)(2,1)}), bf16[8,64,1792]{2,1,0:T(8,128)(2,1)S(1)}, u32[]{:S(2)}, u32[]{:S(2)}) async-start(bf16[8,64,1792]{2,1,0:T(8,128)(2,1)} %bitcast.5), calls=%async_computation.1 | async-start | bytes 3670016 | tf_op jit(solution)/shard_map/all_to_all | solution.py:39
  104.8 48.7 %all-gather.2.cloned.1.call-start = ((), (), s32[]{:S(2)}) async-start(), calls=%async_computation.6 | async-start | bytes 2064384 | tf_op jit(solution)/shard_map/all_gather | solution.py:74
  129.4 15.7 %copy-start.9 = (bf16[7,128,8,128]{3,2,1,0:T(8,128)(2,1)S(1)}, bf16[7,128,8,128]{3,2,1,0:T(8,128)(2,1)}, u32[]{:S(2)}) copy-start(bf16[7,128,8,128]{3,2,1,0:T(8,128)(2,1)} %copy-done.8) | copy-start | bytes 5505028
  145.0 4.1 %copy-start = (bf16[512,896]{1,0:T(8,128)(2,1)}, bf16[512,896]{1,0:T(8,128)(2,1)S(1)}, u32[]{:S(2)}) copy-start(bf16[512,896]{1,0:T(8,128)(2,1)S(1)} %all_gather.6) | copy-start | bytes 2752516
  149.2 33.0 %all-to-all-start.2 = ((bf16[32,16,1024]{2,1,0:T(8,128)(2,1)}), bf16[32,16,1024]{2,1,0:T(8,128)(2,1)S(1)}, u32[]{:S(2)}, u32[]{:S(2)}) async-start(bf16[32,16,1024]{2,1,0:T(8,128)(2,1)} %bitcast.96), calls=%async_computation.2 | async-start | bytes 2097152 | tf_op jit(solution)/shard_map/all_to_all | solution.py:39
  153.5 3.8 %copy-start.4 = (bf16[1024,896]{0,1:T(8,128)(2,1)S(1)}, bf16[1024,896]{0,1:T(8,128)(2,1)}, u32[]{:S(2)}) copy-start(bf16[1024,896]{0,1:T(8,128)(2,1)} %copy.20) | copy-start | bytes 5505028
  153.5 3.8 %copy-start.7 = (bf16[8,128,7,128]{1,0,3,2:T(8,128)(2,1)S(1)}, bf16[8,128,7,128]{1,0,3,2:T(8,128)(2,1)}, u32[]{:S(2)}) copy-start(bf16[8,128,7,128]{1,0,3,2:T(8,128)(2,1)} %copy-done.6) | copy-start | bytes 5505028
  153.5 4.0 %copy-start.14 = (bf16[512,1792]{1,0:T(8,128)(2,1)S(1)}, bf16[512,1792]{1,0:T(8,128)(2,1)}, u32[]{:S(2)}) copy-start(bf16[512,1792]{1,0:T(8,128)(2,1)} %all-gather.2.cloned.1.call-done) | copy-start | bytes 5505028
  182.2 33.9 %all-to-all-start.5 = ((bf16[32,16,1024]{2,1,0:T(8,128)(2,1)}), bf16[32,16,1024]{2,1,0:T(8,128)(2,1)S(1)}, u32[]{:S(2)}, u32[]{:S(2)}) async-start(bf16[32,16,1024]{2,1,0:T(8,128)(2,1)} %bitcast.95), calls=%async_computation.5 | async-start | bytes 2097152 | tf_op jit(solution)/shard_map/all_to_all | solution.py:39
  188.1 1.2 copy-start.1
  192.9 1.5 copy-start.15
  202.2 1.5 copy-start.16
Sparse Core Ops, SparseCore 0:
  130.4 22.2 all-gather.1
where the time goes:
time: 225 us; the launch traced here: 224 us
  waiting for transfers between devices  71.3 us (32%)
  blocking collectives  54.4 us (24%)
  local copies, waits for them, and re-layouts  28.3 us (13%)
  matrix products  28 us (12%)
  starting transfers between devices  23.3 us (10%)
  between operations  14.3 us (6%)
  other arithmetic  4.1 us (2%)
    all_to_all x4, waiting for transfers between devices, reduce_rows(): got = lax.all_to_all(chunks, axis, 0, 0, tiled=False)  53.7 us
    all_to_all x1, blocking collectives, gather_rows(): got = lax.all_to_all(sent, axis, 0, 0, tiled=False)  39.7 us
    unnamed x38, local copies, waits for them, and re-layouts  21.6 us
    all_to_all x4, starting transfers between devices, reduce_rows(): got = lax.all_to_all(chunks, axis, 0, 0, tiled=False)  18 us
    all_to_all x1, waiting for transfers between devices, gather_rows(): got = lax.all_to_all(sent, axis, 0, 0, tiled=False)  17.6 us
    all_gather x1, blocking collectives, shards(): act_full = lax.all_gather(act, 'row', axis=0, tiled=True)  14.7 us
    dot_general x3, matrix products, contract_rows(): lax.dot_general(left, right, (((0,), (0,)), ((), ())), preferred_element_...  10.9 us
    dot_general x3, matrix products, product(): return jnp.dot(left, weight, preferred_element_type=jnp.float32)  8.88 us
  transfers between devices with their start and end apart: 6, of which 5 were waited for; matrix products, arithmetic and copies ran while one was open for 22% of the time, Pallas kernels for 0%

commit v1 on v0

--- a/solution.py
+++ b/solution.py
@@ -2,6 +2,27 @@
 import jax.numpy as jnp
 from jax import lax
 from jax.sharding import PartitionSpec as P
+
+
+def ring_gather(shard, axis, dim):
+    peers, place, width = (lax.axis_size(axis), lax.axis_index(axis), shard.shape[dim])
+    right = [(i, (i + 1) % peers) for i in range(peers)]
+    backward = [(i, (i - 1) % peers) for i in range(peers)]
+    result = jnp.zeros((*shard.shape[:dim], peers * width, *shard.shape[dim + 1 :]), shard.dtype)
+    result = lax.dynamic_update_slice_in_dim(result, shard, place * width, axis=dim)
+    from_left = from_right = shard
+    half = peers // 2
+    for turn in range(1, half + 1):
+        from_left = lax.ppermute(from_left, axis, right)
+        result = lax.dynamic_update_slice_in_dim(
+            result, from_left, (place - turn) % peers * width, axis=dim
+        )
+        if turn < peers - half:
+            from_right = lax.ppermute(from_right, axis, backward)
+            result = lax.dynamic_update_slice_in_dim(
+                result, from_right, (place + turn) % peers * width, axis=dim
+            )
+    return result
 
 
 def masked(weight, mask):
@@ -66,7 +87,7 @@
     up = fwd[:, width:]
     sigma = jax.nn.sigmoid(gate)
     act = (gate * sigma * up).astype(jnp.bfloat16)
-    act_full = lax.all_gather(act, "row", axis=0, tiled=True)
+    act_full = ring_gather(act, "row", 0)
     layer_out = reduce_rows(product(act_full, masked_down), "col", n_col).astype(jnp.bfloat16)
     dact = reduce_rows(product_t(grad_panel, masked_down), "row", n_row)
     dgate = (dact * up * sigma * (1.0 + gate * (1.0 - sigma))).astype(jnp.bfloat16)

time: 225 us -> 232 us (1.031)
  the two profiles are of different devices: /device:TPU:32 before, /device:TPU:6 now
where the time goes in v1:
time: 232 us; the launch traced here: 231 us
  waiting for transfers between devices  78 us (34%)
  blocking collectives  39.9 us (17%)
  starting transfers between devices  36.3 us (16%)
  local copies, waits for them, and re-layouts  29 us (12%)
  matrix products  28.5 us (12%)
  between operations  14.3 us (6%)
  other arithmetic  4.86 us (2%)
    all_to_all x4, waiting for transfers between devices, reduce_rows(): got = lax.all_to_all(chunks, axis, 0, 0, tiled=False)  47.2 us
    all_to_all x1, blocking collectives, gather_rows(): got = lax.all_to_all(sent, axis, 0, 0, tiled=False)  39.9 us
    all_to_all x4, starting transfers between devices, reduce_rows(): got = lax.all_to_all(chunks, axis, 0, 0, tiled=False)  23.9 us
    unnamed x38, local copies, waits for them, and re-layouts  22.1 us
    all_to_all x1, waiting for transfers between devices, gather_rows(): got = lax.all_to_all(sent, axis, 0, 0, tiled=False)  18 us
    ppermute x4, waiting for transfers between devices, ring_gather(): from_left = lax.ppermute(from_left, axis, right)  12.8 us
    dot_general x3, matrix products, contract_rows(): lax.dot_general(left, right, (((0,), (0,)), ((), ())), preferred_element_...  10.9 us
    dot_general x3, matrix products, product(): return jnp.dot(left, weight, preferred_element_type=jnp.float32)  9.39 us
  transfers between devices with their start and end apart: 13, of which 9 were waited for; matrix products, arithmetic and copies ran while one was open for 22% of the time, Pallas kernels for 0%

profile of v1, /device:TPU:6, one launch (start us, length us, event | category | flops | bytes accessed | tf_op | source)
XLA Modules:
  0.0 231.0 jit_solution(17216714909335383678)
XLA Ops:
  7.2 0.9 broadcast_in_dim.8
  8.1 39.9 %all_to_all.30 = bf16[32,16,1024]{2,1,0:T(8,128)(2,1)S(1)} all-to-all(bf16[32,16,1024]{2,1,0:T(8,128)(2,1)S(1)} %broadcast_in_dim.8), channel_id=1, replica_groups=mesh['row'=8,'col'=32] {'col'}, dimensions={0} | all-to-all | bytes 2097152 | tf_op jit(solution)/shard_map/all_to_all | solution.py:52
  48.0 1.1 broadcast_in_dim.7
  49.1 5.2 %all-to-all-start = ((bf16[32,16,1024]{2,1,0:T(8,128)(2,1)}), bf16[32,16,1024]{2,1,0:T(8,128)(2,1)}, u32[]{:S(2)}, u32[]{:S(2)}) async-start(bf16[32,16,1024]{2,1,0:T(8,128)(2,1)} %broadcast_in_dim.7), calls=%async_computation | async-start | bytes 2097152 | tf_op jit(solution)/shard_map/all_to_all | solution.py:52
  54.3 2.4 %copy.20 = bf16[1024,896]{0,1:T(8,128)(2,1)} copy(bf16[1024,896]{1,0:T(8,128)(2,1)S(1)} %copy-done.2) | data formatting | bytes 3670016 | tf_op args[3]
  56.8 3.8 %copy.18 = bf16[1024,896]{0,1:T(8,128)(2,1)} copy(bf16[1024,896]{1,0:T(8,128)(2,1)} %param.8) | data formatting | bytes 3670016 | tf_op args[2]
  60.8 0.3 mul.146
  61.1 1.2 copy-done.8
  62.4 2.2 convolution_convert_fusion.1
  64.6 18.0 %all-to-all-done = bf16[32,16,1024]{2,1,0:T(8,128)(2,1)} async-done(((bf16[32,16,1024]{2,1,0:T(8,128)(2,1)}), bf16[32,16,1024]{2,1,0:T(8,128)(2,1)}, u32[]{:S(2)}, u32[]{:S(2)}) %all-to-all-start) | async-done | bytes 1048608 | tf_op jit(solution)/shard_map/all_to_all | solution.py:52
  82.5 4.9 %all-to-all-start.4 = ((bf16[8,64,896]{2,1,0:T(8,128)(2,1)}), bf16[8,64,896]{2,1,0:T(8,128)(2,1)}, u32[]{:S(2)}, u32[]{:S(2)}) async-start(bf16[8,64,896]{2,1,0:T(8,128)(2,1)} %bitcast.97), calls=%async_computation.4 | async-start | bytes 1835008 | tf_op jit(solution)/shard_map/all_to_all | solution.py:60
  87.8 1.2 copy-done.6
  89.0 2.4 %fusion.4 = bf16[512,896]{0,1:T(8,128)(2,1)S(1)} fusion(bf16[512,1024]{1,0:T(8,128)(2,1)} %bitcast.1, bf16[1024,896]{0,1:T(8,128)(2,1)S(1)} %copy-done.3, bf16[112,8,8,128]{3,2,1,0:T(8,128)(2,1)S(1)} %bitcast.89), kind=kOutput, calls=%fused_computation.18 | convolution fusion | flops 940900352 | bytes 5636096 | tf_op jit(solution)/shard_map/dot_general | solution.py:35
  91.4 0.3 mul.130
  91.7 1.7 copy-done.5
  93.4 2.4 %fusion.3 = bf16[512,896]{0,1:T(8,128)(2,1)S(1)} fusion(bf16[512,1024]{1,0:T(8,128)(2,1)} %bitcast.1, bf16[1024,896]{0,1:T(8,128)(2,1)S(1)} %copy-done.5, bf16[112,8,8,128]{3,2,1,0:T(8,128)(2,1)S(1)} %bitcast.93), kind=kOutput, calls=%fused_computation.17 | convolution fusion | flops 940900352 | bytes 5636096 | tf_op jit(solution)/shard_map/dot_general | solution.py:35
  95.9 2.4 %copy.21 = bf16[512,1792]{1,0:T(8,128)(2,1)} copy(bf16[512,1792]{0,1:T(8,128)(2,1)S(1)} %pad_maximum_fusion) | data formatting | bytes 3670016 | tf_op jit(solution)/shard_map/concatenate | solution.py:76
  98.3 1.7 all-to-all-done.4
  100.0 5.6 %all-to-all-start.1 = ((bf16[8,64,1792]{2,1,0:T(8,128)(2,1)}), bf16[8,64,1792]{2,1,0:T(8,128)(2,1)S(1)}, u32[]{:S(2)}, u32[]{:S(2)}) async-start(bf16[8,64,1792]{2,1,0:T(8,128)(2,1)} %bitcast.5), calls=%async_computation.1 | async-start | bytes 3670016 | tf_op jit(solution)/shard_map/all_to_all | solution.py:60
  105.6 2.0 convert_reduce_fusion.1
  107.7 20.2 %all-to-all-done.1 = bf16[8,64,1792]{2,1,0:T(8,128)(2,1)S(1)} async-done(((bf16[8,64,1792]{2,1,0:T(8,128)(2,1)}), bf16[8,64,1792]{2,1,0:T(8,128)(2,1)S(1)}, u32[]{:S(2)}, u32[]{:S(2)}) %all-to-all-start.1) | async-done | bytes 1835040 | tf_op jit(solution)/shard_map/all_to_all | solution.py:60
  128.1 0.7 copy-done.10
  129.0 0.7 pad_maximum_fusion.1
  129.9 1.7 collective-permute-start.1
  131.6 2.5 %collective-permute-done = bf16[64,896]{1,0:T(8,128)(2,1)S(1)} collective-permute-done((bf16[64,896]{1,0:T(8,128)(2,1)S(1)}, bf16[64,896]{1,0:T(8,128)(2,1)S(1)}, u32[]{:S(2)}, u32[]{:S(2)}) %collective-permute-start) | collective-permute-done | bytes 114720 | tf_op jit(solution)/shard_map/ppermute | solution.py:16
  134.1 1.7 collective-permute-start.3
  135.9 2.4 %collective-permute-done.2 = bf16[64,896]{1,0:T(8,128)(2,1)S(1)} collective-permute-done((bf16[64,896]{1,0:T(8,128)(2,1)S(1)}, bf16[64,896]{1,0:T(8,128)(2,1)S(1)}, u32[]{:S(2)}, u32[]{:S(2)}) %collective-permute-start.2) | collective-permute-done | bytes 114720 | tf_op jit(solution)/shard_map/ppermute | solution.py:16
  138.3 1.7 collective-permute-start.4
  140.1 4.8 %collective-permute-done.4 = bf16[64,896]{1,0:T(8,128)(2,1)S(1)} collective-permute-done((bf16[64,896]{1,0:T(8,128)(2,1)S(1)}, bf16[64,896]{1,0:T(8,128)(2,1)S(1)}, u32[]{:S(2)}, u32[]{:S(2)}) %collective-permute-start.4) | collective-permute-done | bytes 114720 | tf_op jit(solution)/shard_map/ppermute | solution.py:16
  144.9 1.9 collective-permute-start.6
  146.9 3.2 %collective-permute-done.6 = bf16[64,896]{1,0:T(8,128)(2,1)S(1)} collective-permute-done((bf16[64,896]{1,0:T(8,128)(2,1)S(1)}, bf16[64,896]{1,0:T(8,128)(2,1)S(1)}, u32[]{:S(2)}, u32[]{:S(2)}) %collective-permute-start.6) | collective-permute-done | bytes 114720 | tf_op jit(solution)/shard_map/ppermute | solution.py:16
  150.1 4.6 %convolution_convert_fusion = bf16[512,1024]{1,0:T(8,128)(2,1)} fusion(bf16[512,896]{1,0:T(8,128)(2,1)S(1)} %constant_dynamic-update-slice_fusion, bf16[896,1024]{1,0:T(8,128)(2,1)} %param.10, bf16[112,8,8,128]{3,2,1,0:T(8,128)(2,1)} %bitcast.92), kind=kOutput, calls=%fused_computation.13 | convolution fusion | flops 940965888 | bytes 5636096 | tf_op jit(solution)/shard_map/dot_general | solution.py:35
  154.7 5.0 %all-to-all-start.2 = ((bf16[32,16,1024]{2,1,0:T(8,128)(2,1)}), bf16[32,16,1024]{2,1,0:T(8,128)(2,1)S(1)}, u32[]{:S(2)}, u32[]{:S(2)}) async-start(bf16[32,16,1024]{2,1,0:T(8,128)(2,1)} %bitcast.96), calls=%async_computation.2 | async-start | bytes 2097152 | tf_op jit(solution)/shard_map/all_to_all | solution.py:60
  159.8 3.7 %fusion.8 = f32[512,1024]{1,0:T(8,128)S(1)} fusion(bf16[512,1792]{1,0:T(8,128)(2,1)} %all-gather.2.cloned.1.call-done, bf16[1024,896]{0,1:T(8,128)(2,1)} %copy.18, bf16[112,8,8,128]{3,2,1,0:T(8,128)(2,1)} %bitcast.94), kind=kOutput, calls=%fused_computation.22 | convolution fusion | flops 940441600 | bytes 6684672 | tf_op jit(solution)/shard_map/dot_general | solution.py:39
  163.7 2.2 add_convert_fusion
  166.0 19.7 %all-to-all-done.2 = bf16[32,16,1024]{2,1,0:T(8,128)(2,1)S(1)} async-done(((bf16[32,16,1024]{2,1,0:T(8,128)(2,1)}), bf16[32,16,1024]{2,1,0:T(8,128)(2,1)S(1)}, u32[]{:S(2)}, u32[]{:S(2)}) %all-to-all-start.2) | async-done | bytes 1048608 | tf_op jit(solution)/shard_map/all_to_all | solution.py:60
  185.6 8.4 %all-to-all-start.5 = ((bf16[32,16,1024]{2,1,0:T(8,128)(2,1)}), bf16[32,16,1024]{2,1,0:T(8,128)(2,1)S(1)}, u32[]{:S(2)}, u32[]{:S(2)}) async-start(bf16[32,16,1024]{2,1,0:T(8,128)(2,1)} %bitcast.95), calls=%async_computation.5 | async-start | bytes 2097152 | tf_op jit(solution)/shard_map/all_to_all | solution.py:60
  194.6 0.9 copy-done.1
  195.5 2.8 %fusion = bf16[896,1024]{1,0:T(8,128)(2,1)} fusion(f32[112,8,8,128]{3,2,1,0:T(8,128)S(1)} %bitcast.84, bf16[512,896]{1,0:T(8,128)(2,1)S(1)} %copy-done.1, bf16[512,1024]{1,0:T(8,128)(2,1)S(1)} %bitcast.86), kind=kOutput, calls=%fused_computation.1 | convolution fusion | flops 942276608 | bytes 7471104 | tf_op jit(solution)/shard_map/dot_general | solution.py:45
  198.3 0.8 reduce_sum.43
  199.4 1.2 copy-done.15
  200.6 4.0 %fusion.2 = bf16[1024,896]{0,1:T(8,128)(2,1)} fusion(f32[112,8,8,128]{3,2,1,0:T(8,128)S(1)} %bitcast.88, bf16[512,1024]{1,0:T(8,128)(2,1)} %bitcast.1, bf16[512,1792]{1,0:T(8,128)(2,1)S(1)} %copy-done.15), kind=kOutput, calls=%fused_computation.5 | convolution fusion | flops 942276608 | bytes 7471104 | tf_op jit(solution)/shard_map/dot_general | solution.py:45
  204.6 3.8 %copy.26 = bf16[1024,896]{1,0:T(8,128)(2,1)} copy(bf16[1024,896]{0,1:T(8,128)(2,1)} %fusion.2) | data formatting | bytes 3670016
  208.7 1.2 copy-done.16
  209.9 4.1 %fusion.1 = bf16[1024,896]{0,1:T(8,128)(2,1)} fusion(f32[112,8,8,128]{3,2,1,0:T(8,128)S(1)} %bitcast.87, bf16[512,1024]{1,0:T(8,128)(2,1)} %bitcast.1, bf16[512,1792]{1,0:T(8,128)(2,1)S(1)} %copy-done.16), kind=kOutput, calls=%fused_computation.3 | convolution fusion | flops 942276608 | bytes 7471104 | tf_op jit(solution)/shard_map/dot_general | solution.py:45
  214.0 3.8 %copy.27 = bf16[1024,896]{1,0:T(8,128)(2,1)} copy(bf16[1024,896]{0,1:T(8,128)(2,1)} %fusion.1) | data formatting | bytes 3670016
  217.8 5.6 %all-to-all-done.5 = bf16[32,16,1024]{2,1,0:T(8,128)(2,1)S(1)} async-done(((bf16[32,16,1024]{2,1,0:T(8,128)(2,1)}), bf16[32,16,1024]{2,1,0:T(8,128)(2,1)S(1)}, u32[]{:S(2)}, u32[]{:S(2)}) %all-to-all-start.5) | async-done | bytes 1048608 | tf_op jit(solution)/shard_map/all_to_all | solution.py:60
  223.4 0.8 reduce_sum.45
  (59 shorter events, 2.8 us)
Async XLA Ops:
  7.2 40.8 %copy-start.11 = (bf16[16,1024]{1,0:T(8,128)(2,1)S(1)}, bf16[16,1024]{1,0:T(8,128)(2,1)}, u32[]{:S(2)}) copy-start(bf16[16,1024]{1,0:T(8,128)(2,1)} %param.6) | copy-start | bytes 98308
  48.0 6.3 %copy-start.2 = (bf16[1024,896]{1,0:T(8,128)(2,1)S(1)}, bf16[1024,896]{1,0:T(8,128)(2,1)}, u32[]{:S(2)}) copy-start(bf16[1024,896]{1,0:T(8,128)(2,1)} %param.9) | copy-start | bytes 5505028
  49.1 33.5 %all-to-all-start = ((bf16[32,16,1024]{2,1,0:T(8,128)(2,1)}), bf16[32,16,1024]{2,1,0:T(8,128)(2,1)}, u32[]{:S(2)}, u32[]{:S(2)}) async-start(bf16[32,16,1024]{2,1,0:T(8,128)(2,1)} %broadcast_in_dim.7), calls=%async_computation | async-start | bytes 2097152 | tf_op jit(solution)/shard_map/all_to_all | solution.py:52
  54.3 2.4 %copy-start.12 = (s32[3,8,7]{2,1,0:T(8,128)S(1)}, s32[3,8,7]{2,1,0:T(8,128)}, u32[]{:S(2)}) copy-start(s32[3,8,7]{2,1,0:T(8,128)} %param.11) | copy-start | bytes 2020
  60.6 1.8 copy-start.13
  61.1 1.3 copy-start.8
  82.5 6.4 %copy-start.3 = (bf16[1024,896]{0,1:T(8,128)(2,1)S(1)}, bf16[1024,896]{0,1:T(8,128)(2,1)}, u32[]{:S(2)}) copy-start(bf16[1024,896]{0,1:T(8,128)(2,1)} %copy.20) | copy-start | bytes 5505028
  82.5 17.5 %all-to-all-start.4 = ((bf16[8,64,896]{2,1,0:T(8,128)(2,1)}), bf16[8,64,896]{2,1,0:T(8,128)(2,1)}, u32[]{:S(2)}, u32[]{:S(2)}) async-start(bf16[8,64,896]{2,1,0:T(8,128)(2,1)} %bitcast.97), calls=%async_computation.4 | async-start | bytes 1835008 | tf_op jit(solution)/shard_map/all_to_all | solution.py:60
  87.8 1.2 copy-start.6
  91.4 2.0 copy-start.5
  91.7 4.1 %copy-start.9 = (bf16[8,128,7,128]{1,0,3,2:T(8,128)(2,1)}, bf16[8,128,7,128]{1,0,3,2:T(8,128)(2,1)S(1)}, u32[]{:S(2)}) copy-start(bf16[8,128,7,128]{1,0,3,2:T(8,128)(2,1)S(1)} %mul.130) | copy-start | bytes 5505028
  100.0 27.9 %all-to-all-start.1 = ((bf16[8,64,1792]{2,1,0:T(8,128)(2,1)}), bf16[8,64,1792]{2,1,0:T(8,128)(2,1)S(1)}, u32[]{:S(2)}, u32[]{:S(2)}) async-start(bf16[8,64,1792]{2,1,0:T(8,128)(2,1)} %bitcast.5), calls=%async_computation.1 | async-start | bytes 3670016 | tf_op jit(solution)/shard_map/all_to_all | solution.py:60
  105.6 54.1 %all-gather.2.cloned.1.call-start = ((), (), s32[]{:S(2)}) async-start(), calls=%async_computation.6 | async-start | bytes 2064384 | tf_op jit(solution)/shard_map/all_gather | solution.py:95
  127.9 0.9 copy-start.10
  129.9 4.2 %collective-permute-start = (bf16[64,896]{1,0:T(8,128)(2,1)S(1)}, bf16[64,896]{1,0:T(8,128)(2,1)S(1)}, u32[]{:S(2)}, u32[]{:S(2)}) collective-permute-start(bf16[64,896]{1,0:T(8,128)(2,1)S(1)} %get-tuple-element.16), channel_id=1, source_target_pairs={{0,32},{32,64},{64,96},{96,128},{128,160},{160,192},{192,224},{224... | collective-permute-start | bytes 344072 | tf_op jit(solution)/shard_map/ppermute | solution.py:16
  129.9 4.2 %collective-permute-start.1 = (bf16[64,896]{1,0:T(8,128)(2,1)S(1)}, bf16[64,896]{1,0:T(8,128)(2,1)S(1)}, u32[]{:S(2)}, u32[]{:S(2)}) collective-permute-start(bf16[64,896]{1,0:T(8,128)(2,1)S(1)} %get-tuple-element.16), channel_id=1, source_target_pairs={{0,224},{32,0},{64,32},{96,64},{128,96},{160,128},{192,160},{224,1... | collective-permute-start | bytes 344072 | tf_op jit(solution)/shard_map/ppermute | solution.py:21
  134.1 4.2 %collective-permute-start.2 = (bf16[64,896]{1,0:T(8,128)(2,1)S(1)}, bf16[64,896]{1,0:T(8,128)(2,1)S(1)}, u32[]{:S(2)}, u32[]{:S(2)}) collective-permute-start(bf16[64,896]{1,0:T(8,128)(2,1)S(1)} %collective-permute-done), channel_id=1, source_target_pairs={{0,32},{32,64},{64,96},{96,128},{128,160},{160,192},{192,224},{224... | collective-permute-start | bytes 344072 | tf_op jit(solution)/shard_map/ppermute | solution.py:16
  134.1 6.0 %collective-permute-start.3 = (bf16[64,896]{1,0:T(8,128)(2,1)S(1)}, bf16[64,896]{1,0:T(8,128)(2,1)S(1)}, u32[]{:S(2)}, u32[]{:S(2)}) collective-permute-start(bf16[64,896]{1,0:T(8,128)(2,1)S(1)} %collective-permute-done.1), channel_id=1, source_target_pairs={{0,224},{32,0},{64,32},{96,64},{128,96},{160,128},{192,160},{224,1... | collective-permute-start | bytes 344072 | tf_op jit(solution)/shard_map/ppermute | solution.py:21
  138.3 6.6 %collective-permute-start.4 = (bf16[64,896]{1,0:T(8,128)(2,1)S(1)}, bf16[64,896]{1,0:T(8,128)(2,1)S(1)}, u32[]{:S(2)}, u32[]{:S(2)}) collective-permute-start(bf16[64,896]{1,0:T(8,128)(2,1)S(1)} %collective-permute-done.2), channel_id=1, source_target_pairs={{0,32},{32,64},{64,96},{96,128},{128,160},{160,192},{192,224},{224... | collective-permute-start | bytes 344072 | tf_op jit(solution)/shard_map/ppermute | solution.py:16
  140.1 6.8 %collective-permute-start.5 = (bf16[64,896]{1,0:T(8,128)(2,1)S(1)}, bf16[64,896]{1,0:T(8,128)(2,1)S(1)}, u32[]{:S(2)}, u32[]{:S(2)}) collective-permute-start(bf16[64,896]{1,0:T(8,128)(2,1)S(1)} %collective-permute-done.3), channel_id=1, source_target_pairs={{0,224},{32,0},{64,32},{96,64},{128,96},{160,128},{192,160},{224,1... | collective-permute-start | bytes 344072 | tf_op jit(solution)/shard_map/ppermute | solution.py:21
  144.9 5.1 %collective-permute-start.6 = (bf16[64,896]{1,0:T(8,128)(2,1)S(1)}, bf16[64,896]{1,0:T(8,128)(2,1)S(1)}, u32[]{:S(2)}, u32[]{:S(2)}) collective-permute-start(bf16[64,896]{1,0:T(8,128)(2,1)S(1)} %collective-permute-done.4), channel_id=1, source_target_pairs={{0,32},{32,64},{64,96},{96,128},{128,160},{160,192},{192,224},{224... | collective-permute-start | bytes 344072 | tf_op jit(solution)/shard_map/ppermute | solution.py:16
  150.1 4.7 %copy-start = (bf16[512,896]{1,0:T(8,128)(2,1)}, bf16[512,896]{1,0:T(8,128)(2,1)S(1)}, u32[]{:S(2)}) copy-start(bf16[512,896]{1,0:T(8,128)(2,1)S(1)} %constant_dynamic-update-slice_fusion) | copy-start | bytes 2752516
  154.7 30.9 %all-to-all-start.2 = ((bf16[32,16,1024]{2,1,0:T(8,128)(2,1)}), bf16[32,16,1024]{2,1,0:T(8,128)(2,1)S(1)}, u32[]{:S(2)}, u32[]{:S(2)}) async-start(bf16[32,16,1024]{2,1,0:T(8,128)(2,1)} %bitcast.96), calls=%async_computation.2 | async-start | bytes 2097152 | tf_op jit(solution)/shard_map/all_to_all | solution.py:60
  159.8 3.8 %copy-start.4 = (bf16[1024,896]{0,1:T(8,128)(2,1)S(1)}, bf16[1024,896]{0,1:T(8,128)(2,1)}, u32[]{:S(2)}) copy-start(bf16[1024,896]{0,1:T(8,128)(2,1)} %copy.20) | copy-start | bytes 5505028
  159.8 3.8 %copy-start.7 = (bf16[8,128,7,128]{1,0,3,2:T(8,128)(2,1)S(1)}, bf16[8,128,7,128]{1,0,3,2:T(8,128)(2,1)}, u32[]{:S(2)}) copy-start(bf16[8,128,7,128]{1,0,3,2:T(8,128)(2,1)} %copy-done.6) | copy-start | bytes 5505028
  159.8 4.0 %copy-start.14 = (bf16[512,1792]{1,0:T(8,128)(2,1)S(1)}, bf16[512,1792]{1,0:T(8,128)(2,1)}, u32[]{:S(2)}) copy-start(bf16[512,1792]{1,0:T(8,128)(2,1)} %all-gather.2.cloned.1.call-done) | copy-start | bytes 5505028
  185.6 37.7 %all-to-all-start.5 = ((bf16[32,16,1024]{2,1,0:T(8,128)(2,1)}), bf16[32,16,1024]{2,1,0:T(8,128)(2,1)S(1)}, u32[]{:S(2)}, u32[]{:S(2)}) async-start(bf16[32,16,1024]{2,1,0:T(8,128)(2,1)} %bitcast.95), calls=%async_computation.5 | async-start | bytes 2097152 | tf_op jit(solution)/shard_map/all_to_all | solution.py:60
  194.3 1.2 copy-start.1
  199.1 1.5 copy-start.15
  208.4 1.5 copy-start.16
Sparse Core Ops, SparseCore 0:
  129.8 23.0 all-gather.1
